TPU v7x, 256 devices: a whole 4x4x8 slice. The times are simulated.
256 devices in a mesh: gx: 4 (over z_lo), gy: 8 (over z_hi, y), gz: 8 (over x, core).
Axes of the slice: x: 4, y: 4, z: 8 (z_hi: 2, z_lo: 4; z = z_hi * 4 + z_lo), core: 2. Of those that a mesh axis runs over, the one named last changes fastest.
Arguments:
- vectors: float32 [4, 5, 125, 4, 8, 1024], P(None, None, None, 'gx', 'gy', 'gz'), may hold values from -6 to 6
- stiffness: float32 [5, 5], replicated, may hold values from -2.5 to 2.5
- flux: float32 [3, 5, 5], replicated, may hold values from -1.25 to 1.25
- penalty: float32 [3, 5], replicated, may hold values from 0.2 to 2
- local_factor: float32 [5, 5], replicated, may hold values from -2.5 to 2.5
- element_field_factor: float32 [5, 5], replicated, may hold values from -2.5 to 2.5
- aggregate: int32 [4, 8, 1024], P('gx', 'gy', 'gz'), may hold values from 0 to 1023
- coarse_inverse: float32 [20480, 5120], P(('gx', 'gy', 'gz')), may hold values from -0.078125 to 0.078125
Outputs:
- result: float32 [4, 5, 125, 4, 8, 1024], P(None, None, None, 'gx', 'gy', 'gz')
Inputs may be any that keep to these rules, and one draw needn't show every extreme that they name: aggregate numbers are counted within the elements of one index of gx.
All inputs are finite; a program needn't handle non-finite values.
Results may differ from a plain program's by a relative error of at most 0.0001.
Values sent between devices are 32-bit elements; how exact they have to be, the bound alone decides.
No kernel may reach another device: no remote copies, remote signals or barrier semaphores. Data moves between devices by JAX's collectives and lax.ppermute only.
A program may use at most 256 MiB of HBM per device.

v0:
```python
import jax
import jax.numpy as jnp
import numpy as np
from jax import lax
from jax.sharding import PartitionSpec as P

HIGH = lax.Precision.HIGHEST


def with_halo(shard, sides, width):
    for axis, dim in sides:
        size, length = (lax.axis_size(axis), shard.shape[dim])
        up = [(i, (i + 1) % size) for i in range(size - 1)]
        down = [(j, i) for i, j in up]
        last = lax.slice_in_dim(shard, length - width, length, axis=dim)
        initial = lax.slice_in_dim(shard, 0, width, axis=dim)
        before = lax.ppermute(last, axis, up)
        after = lax.ppermute(initial, axis, down)
        shard = jnp.concatenate([before, shard, after], axis=dim)
    return shard


def kron_three(first, second, third):
    return jnp.kron(jnp.kron(first, second), third)


def operator_matrix(stiffness, flux):
    unit = jnp.eye(5, dtype=jnp.float32)
    sweeps = [
        kron_three(stiffness, unit, unit),
        kron_three(unit, stiffness, unit),
        kron_three(unit, unit, stiffness),
    ]
    total = jnp.zeros((625, 625), jnp.float32)
    for axis in range(3):
        total = total + jnp.kron(flux[axis], sweeps[axis])
    return total.reshape(5, 125, 5, 125)


def face_table():
    table = np.zeros((150, 125), np.float32)
    for axis in range(3):
        for side in range(2):
            level = 4 * side
            for first in range(5):
                for second in range(5):
                    if axis == 0:
                        node = 25 * level + 5 * first + second
                    elif axis == 1:
                        node = 25 * first + 5 * level + second
                    else:
                        node = 25 * first + 5 * second + level
                    table[50 * axis + 25 * side + 5 * first + second, node] = 1.0
    return table


def operate(flat, dims, big, penalty, selects):
    vecs, fields, elements = (flat.shape[0], flat.shape[1], flat.shape[3])
    output = flat + jnp.einsum("fqgp,kgpe->kfqe", big, flat, precision=HIGH)
    faces = jnp.einsum("sq,kfqe->kfse", selects, flat, precision=HIGH)
    shaped = (vecs, fields, 25) + dims
    pairs = []
    for axis in range(3):
        minus = faces[:, :, 50 * axis : 50 * axis + 25].reshape(shaped)
        plus = faces[:, :, 50 * axis + 25 : 50 * axis + 50].reshape(shaped)
        pairs.append((minus, plus))
    neighbours = []
    stacks = [jnp.stack([pairs[axis][0], pairs[axis][1]], 0) for axis in range(3)]
    outer = [
        with_halo(stacks[0], (("gx", 4),), 1),
        with_halo(stacks[1], (("gy", 5),), 1),
        with_halo(stacks[2], (("gz", 6),), 1),
    ]
    for axis in range(3):
        count = dims[axis]
        after = lax.slice_in_dim(outer[axis][0], 2, count + 2, axis=3 + axis)
        before = lax.slice_in_dim(outer[axis][1], 0, count, axis=3 + axis)
        neighbours.append((after, before))
    terms = []
    for axis in range(3):
        minus, plus = pairs[axis]
        tau = penalty[axis][None, :, None, None, None, None]
        terms.append((tau * (minus - neighbours[axis][1])).reshape(vecs, fields, 25, elements))
        terms.append((tau * (plus - neighbours[axis][0])).reshape(vecs, fields, 25, elements))
    stacked = jnp.concatenate(terms, axis=2)
    return output + jnp.einsum("sq,kfse->kfqe", selects, stacked, precision=HIGH)


def precondition(flat, local_kron, element_field_factor, onehot, coarse_inverse):
    vecs, fields, elements = (flat.shape[0], flat.shape[1], flat.shape[3])
    fine = jnp.einsum("qp,kfpe->kfqe", local_kron, flat, precision=HIGH)
    fine = jnp.einsum("fg,kgqe->kfqe", element_field_factor, fine, precision=HIGH)
    nagg = coarse_inverse.shape[1] // fields
    means = jnp.sum(flat, axis=2) * (1.0 / 125.0)
    block = means.reshape(vecs * fields, elements)
    partial_sum = jnp.dot(block, onehot, precision=HIGH)
    restricted = lax.psum(partial_sum, ("gy", "gz"))
    merged = restricted.reshape(vecs, fields * nagg)
    owned = jnp.einsum("kc,rc->kr", merged, coarse_inverse, precision=HIGH)
    coarse = lax.all_gather(owned, ("gy", "gz"), axis=1, tiled=True)
    values = jnp.dot(coarse.reshape(vecs * fields, nagg), onehot.T, precision=HIGH)
    back = values.reshape(vecs, fields, elements)
    return fine + back[:, :, None, :]


def on_device(
    vectors, stiffness, flux, penalty, local_factor, element_field_factor, aggregate, coarse_inverse
):
    big = operator_matrix(stiffness, flux)
    local_kron = kron_three(local_factor, local_factor, local_factor)
    selects = jnp.asarray(face_table())
    dims = tuple(vectors.shape[3:])
    elements = aggregate.size
    nagg = coarse_inverse.shape[1] // vectors.shape[1]
    onehot = (
        aggregate.reshape(elements)[:, None] == jnp.arange(nagg, dtype=jnp.int32)[None, :]
    ).astype(jnp.float32)
    flat = vectors.reshape(vectors.shape[:3] + (elements,))
    for turn in range(2):
        flat = precondition(flat, local_kron, element_field_factor, onehot, coarse_inverse)
        flat = operate(flat, dims, big, penalty, selects)
    return flat.reshape(vectors.shape)


def solution(mesh):
    placed = (
        P(None, None, None, "gx", "gy", "gz"),
        P(),
        P(),
        P(),
        P(),
        P(),
        P("gx", "gy", "gz"),
        P(("gx", "gy", "gz"), None),
    )
    return jax.shard_map(
        on_device,
        mesh=mesh,
        in_specs=placed,
        out_specs=P(None, None, None, "gx", "gy", "gz"),
        check_vma=False,
    )
```

profile of v0, /device:TPU:225, one launch (start us, length us, event | category | flops | bytes accessed | tf_op | source)
XLA Modules:
  0.0 1826.5 jit_solution(4462123117621494507)
XLA Ops:
  6.5 2.1 reduce_sum.18
  10.7 1.7 broadcast_multiply_fusion.3
  12.3 2.8 reshape.385
  15.1 2.5 convolution_bitcast_fusion.3
  18.1 1.7 broadcast_multiply_fusion
  19.8 2.6 broadcast_multiply_fusion.2
  23.6 3.4 mul.353
  27.0 3.4 mul.364
  30.4 3.4 mul.374
  34.4 687.8 %all-reduce.3.cloned.1.call-done = f32[4,5120]{1,0:T(4,128)} async-done(((f32[4,5120]{1,0:T(4,128)}), f32[4,5120]{1,0:T(4,128)}) %all-reduce.3.cloned.1.call-update) | async-done | bytes 81936 | tf_op jit(solution)/shard_map/psum | solution.py:97
  722.2 2.3 convolution_bitcast_fusion.5
  724.4 117.8 %all-gather = f32[64,80,4]{1,2,0:T(4,128)S(1)} all-gather(f32[1,80,4]{1,2,0:T(4,128)S(1)} %convolution_bitcast_fusion.5), channel_id=1, replica_groups=mesh['gx'=4,'gy'=8,'gz'=8] {'gy','gz'}, dimensions={0}, use_global_device_ids=true | all-gather | bytes 83200 | tf_op jit(solution)/shard_map/all_gather | solution.py:100
  842.9 2.5 bitcast_add_fusion.5
  846.8 1.6 convolution_bitcast_fusion.1
  850.6 1.9 collective-permute-start.2
  852.5 9.4 collective-permute-start.3
  863.2 2.0 copy.64
  865.2 1.9 collective-permute-start.4
  867.1 2.0 copy.65
  869.1 2.5 collective-permute-start.5
  871.7 2.1 fusion.75
  876.3 4.6 fusion.9
  880.9 5.0 collective-permute-start.1
  887.1 1.9 copy.67
  889.0 2.1 pad_maximum_fusion.4
  893.5 2.8 collective-permute-done
  901.6 9.2 concatenate.27
  910.8 2.4 fusion.78
  913.2 4.3 fusion.76
  918.6 3.8 convolution_bitcast_fusion.2
  922.4 1.8 copy.70
  924.2 700.6 %all-reduce.5.cloned.1.call-done = f32[4,5120]{1,0:T(4,128)} async-done(((f32[4,5120]{1,0:T(4,128)}), f32[4,5120]{1,0:T(4,128)}) %all-reduce.5.cloned.1.call-update) | async-done | bytes 81936 | tf_op jit(solution)/shard_map/psum | solution.py:97
  1624.9 2.3 convolution_bitcast_fusion.4
  1627.1 118.0 %all-gather.1 = f32[64,80,4]{1,2,0:T(4,128)S(1)} all-gather(f32[1,80,4]{1,2,0:T(4,128)S(1)} %convolution_bitcast_fusion.4), channel_id=1, replica_groups=mesh['gx'=4,'gy'=8,'gz'=8] {'gy','gz'}, dimensions={0}, use_global_device_ids=true | all-gather | bytes 83200 | tf_op jit(solution)/shard_map/all_gather | solution.py:100
  1745.8 3.5 bitcast_add_fusion.2
  1753.7 1.9 collective-permute-start.8
  1755.6 9.4 collective-permute-start.9
  1770.2 1.9 collective-permute-start.10
  1773.6 2.4 collective-permute-start.11
  1776.0 6.2 fusion.12
  1782.2 5.0 collective-permute-start.7
  1789.6 2.0 pad_maximum_fusion.5
  1793.9 5.4 collective-permute-done.6
  1804.1 3.3 concatenate.31
  1807.5 4.3 fusion.79
  1811.7 1.8 copy.88
  1813.6 3.6 fusion
  1817.2 2.4 copy.89
  (159 shorter events, 43.0 us)
Async XLA Ops:
  6.5 715.7 %copy-start = (f32[80,5120]{1,0:T(8,128)S(1)}, f32[80,5120]{1,0:T(8,128)}, u32[]{:S(2)}) copy-start(f32[80,5120]{1,0:T(8,128)} %param.16) | copy-start | bytes 4915204
  6.5 3.9 copy-start.22
  6.5 715.7 %all-reduce.3.cloned.1.call-start = ((), (), s32[]{:S(2)}) async-start(), calls=%async_computation | async-start | bytes 163840 | tf_op jit(solution)/shard_map/psum | solution.py:97
  10.4 1614.5 %all-reduce.5.cloned.1.call-start = ((), (), s32[]{:S(2)}) async-start(), calls=%async_computation.1 | async-start | bytes 163840 | tf_op jit(solution)/shard_map/psum | solution.py:97
  15.1 3.0 copy-start.14
  15.1 2.6 copy-start.23
  15.1 2.9 copy-start.27
  19.8 3.2 copy-start.36
  23.6 876.7 %copy-start.25 = (f32[5]{0:T(128)}, f32[5]{0:T(128)S(1)}, u32[]{:S(2)}) copy-start(f32[5]{0:T(128)S(1)} %get-tuple-element.63) | copy-start | bytes 64
  23.6 876.7 %copy-start.28 = (f32[5]{0:T(128)}, f32[5]{0:T(128)S(1)}, u32[]{:S(2)}) copy-start(f32[5]{0:T(128)S(1)} %get-tuple-element.62) | copy-start | bytes 64
  33.8 808.6 %copy-start.37 = (s32[1,1,128]{2,1,0:T(1,128)S(1)}, s32[1,1,128]{2,1,0:T(1,128)}, u32[]{:S(2)}) copy-start(s32[1,1,128]{2,1,0:T(1,128)} %param.15) | copy-start | bytes 1540
  33.9 809.0 %copy-start.24 = (f32[5,5]{1,0:T(8,128)S(1)}, f32[5,5]{1,0:T(8,128)}, u32[]{:S(2)}) copy-start(f32[5,5]{1,0:T(8,128)} %param.14) | copy-start | bytes 304
  842.9 3.9 copy-start.12
  845.4 1.3 copy-start.3
  849.4 13.8 copy-start.6
  849.4 13.8 copy-start.9
  849.4 13.8 copy-start.10
  850.6 40.6 %collective-permute-start.2 = (f32[2,4,5,25,1,1,128]{6,1,5,4,3,2,0:T(4,128)}, f32[2,4,5,25,1,1,128]{6,1,5,4,3,2,0:T(4,128)}, u32[]{:S(2)}, u32[]{:S(2)}) collective-permute-start(f32[2,4,5,25,1,1,128]{6,1,5,4,3,2,0:T(4,128)} %copy.60), channel_id=1, source_target_pairs={{0,8},{8,16},{16,24},{24,32},{32,40},{40,48},{48,56},{1,9},{9,17},... | collective-permute-start | bytes 1536008 | tf_op jit(solution)/shard_map/ppermute | solution.py:17
  852.5 39.8 %collective-permute-start.3 = (f32[2,4,5,25,1,1,128]{6,1,5,4,3,2,0:T(4,128)}, f32[2,4,5,25,1,1,128]{6,1,5,4,3,2,0:T(4,128)}, u32[]{:S(2)}, u32[]{:S(2)}) collective-permute-start(f32[2,4,5,25,1,1,128]{6,1,5,4,3,2,0:T(4,128)} %copy.60), channel_id=1, source_target_pairs={{8,0},{16,8},{24,16},{32,24},{40,32},{48,40},{56,48},{9,1},{17,9},... | collective-permute-start | bytes 1536008 | tf_op jit(solution)/shard_map/ppermute | solution.py:18
  865.2 15.7 collective-permute-start.4
  869.1 7.1 copy-start.4
  869.1 7.1 copy-start.16
  869.1 7.1 copy-start.18
  869.1 7.1 copy-start.20
  869.1 7.1 copy-start.32
  869.1 7.1 copy-start.34
  869.1 7.1 copy-start.35
  869.1 17.9 collective-permute-start.5
  874.9 21.4 %collective-permute-start = (f32[2,4,5,25,1,1,128]{6,1,5,4,3,2,0:T(4,128)}, f32[2,4,5,25,1,1,128]{6,1,5,4,3,2,0:T(4,128)}, u32[]{:S(2)}, u32[]{:S(2)}) collective-permute-start(f32[2,4,5,25,1,1,128]{6,1,5,4,3,2,0:T(4,128)} %copy.54), channel_id=1, source_target_pairs={{0,64},{64,128},{128,192},{1,65},{65,129},{129,193},{2,66},{66,130... | collective-permute-start | bytes 1536008 | tf_op jit(solution)/shard_map/ppermute | solution.py:17
  880.9 17.0 collective-permute-start.1
  891.1 6.2 copy-start.7
  897.6 1.4 copy-start.11
  910.8 2.4 copy-start.5
  913.2 4.3 copy-start.38
  913.2 5.3 copy-start.15
  1745.8 4.8 copy-start.13
  1752.5 15.0 copy-start.8
  1753.7 38.0 %collective-permute-start.8 = (f32[2,4,5,25,1,1,128]{6,1,5,4,3,2,0:T(4,128)}, f32[2,4,5,25,1,1,128]{6,1,5,4,3,2,0:T(4,128)}, u32[]{:S(2)}, u32[]{:S(2)}) collective-permute-start(f32[2,4,5,25,1,1,128]{6,1,5,4,3,2,0:T(4,128)} %copy.80), channel_id=1, source_target_pairs={{0,8},{8,16},{16,24},{24,32},{32,40},{40,48},{48,56},{1,9},{9,17},... | collective-permute-start | bytes 1536008 | tf_op jit(solution)/shard_map/ppermute | solution.py:17
  1755.6 37.2 %collective-permute-start.9 = (f32[2,4,5,25,1,1,128]{6,1,5,4,3,2,0:T(4,128)}, f32[2,4,5,25,1,1,128]{6,1,5,4,3,2,0:T(4,128)}, u32[]{:S(2)}, u32[]{:S(2)}) collective-permute-start(f32[2,4,5,25,1,1,128]{6,1,5,4,3,2,0:T(4,128)} %copy.80), channel_id=1, source_target_pairs={{8,0},{16,8},{24,16},{32,24},{40,32},{48,40},{56,48},{9,1},{17,9},... | collective-permute-start | bytes 1536008 | tf_op jit(solution)/shard_map/ppermute | solution.py:18
  1766.2 33.2 %collective-permute-start.6 = (f32[2,4,5,25,1,1,128]{6,1,5,4,3,2,0:T(4,128)}, f32[2,4,5,25,1,1,128]{6,1,5,4,3,2,0:T(4,128)}, u32[]{:S(2)}, u32[]{:S(2)}) collective-permute-start(f32[2,4,5,25,1,1,128]{6,1,5,4,3,2,0:T(4,128)} %copy.75), channel_id=1, source_target_pairs={{0,64},{64,128},{128,192},{1,65},{65,129},{129,193},{2,66},{66,130... | collective-permute-start | bytes 1536008 | tf_op jit(solution)/shard_map/ppermute | solution.py:17
  1767.5 8.5 copy-start.17
  1767.5 8.5 copy-start.19
  1767.5 8.5 copy-start.21
  1767.5 8.5 copy-start.33
  1770.2 11.9 collective-permute-start.10
  1773.6 14.8 collective-permute-start.11
  1782.2 18.7 %collective-permute-start.7 = (f32[2,4,5,25,1,1,128]{6,1,5,4,3,2,0:T(4,128)}, f32[2,4,5,25,1,1,128]{6,1,5,4,3,2,0:T(4,128)}, u32[]{:S(2)}, u32[]{:S(2)}) collective-permute-start(f32[2,4,5,25,1,1,128]{6,1,5,4,3,2,0:T(4,128)} %copy.75), channel_id=1, source_target_pairs={{64,0},{128,64},{192,128},{65,1},{129,65},{193,129},{66,2},{130,66... | collective-permute-start | bytes 1536008 | tf_op jit(solution)/shard_map/ppermute | solution.py:18
  1813.6 6.0 copy-start.1
  (5 other events, 4.4 us)
Sparse Core Ops, SparseCore 0:
  10.5 711.6 all-reduce.2
  918.7 706.1 all-reduce.4
where the time goes:
time: 1840 us; the launch traced here: 1830 us
  waiting for transfers between devices  1400 us (76%)
  blocking collectives  236 us (13%)
  local copies, waits for them, and re-layouts  67.1 us (4%)
  starting transfers between devices  43.9 us (2%)
  matrix products  39.6 us (2%)
  other arithmetic  29 us (2%)
    psum x2, waiting for transfers between devices, precondition(): restricted = lax.psum(partial_sum, ('gy', 'gz'))  1390 us
    all_gather x2, blocking collectives, precondition(): coarse = lax.all_gather(owned, ('gy', 'gz'), axis=1, tiled=True)  236 us
  transfers between devices with their start and end apart: 14, of which 4 were waited for; matrix products, arithmetic and copies ran while one was open for 4% of the time, Pallas kernels for 0%

commit v1 on v0

--- a/solution.py
+++ b/solution.py
@@ -97,7 +97,10 @@
     restricted = lax.psum(partial_sum, ("gy", "gz"))
     merged = restricted.reshape(vecs, fields * nagg)
     owned = jnp.einsum("kc,rc->kr", merged, coarse_inverse, precision=HIGH)
-    coarse = lax.all_gather(owned, ("gy", "gz"), axis=1, tiled=True)
+    carry = lax.axis_size(("gy", "gz"))
+    field_out = jnp.stack(carry * [owned], axis=0)
+    tall = lax.all_to_all(field_out, ("gy", "gz"), 0, 0)
+    coarse = jnp.concatenate(tall, 1)
     values = jnp.dot(coarse.reshape(vecs * fields, nagg), onehot.T, precision=HIGH)
     back = values.reshape(vecs, fields, elements)
     return fine + back[:, :, None, :]

time: 1840 us -> 1650 us (0.90)
  blocking collectives: 236 us -> 0 us
  starting transfers between devices: 43.9 us -> 71.1 us
    all_gather x2 -> x0, blocking collectives: 236 us -> none  [precondition(): coarse = lax.all_gather(owned, ('gy', 'gz'), axis=1, tiled=True)]
    all_to_all x0 -> x2, starting transfers between devices: none -> 24.9 us  [precondition(): tall = lax.all_to_all(field_out, ('gy', 'gz'), 0, 0)]
  transfers between devices with their start and end apart: 14 -> 16, of which waited for: 4 -> 6; matrix products, arithmetic and copies ran while one was open for 4% -> 4% of each run, Pallas kernels for 0% -> 0%
where the time goes in v1:
time: 1650 us; the launch traced here: 1640 us
  waiting for transfers between devices  1410 us (85%)
  starting transfers between devices  71.1 us (4%)
  local copies, waits for them, and re-layouts  68.3 us (4%)
  matrix products  39.7 us (2%)
  other arithmetic  28.9 us (2%)
    psum x2, waiting for transfers between devices, precondition(): restricted = lax.psum(partial_sum, ('gy', 'gz'))  1400 us
  transfers between devices with their start and end apart: 16, of which 6 were waited for; matrix products, arithmetic and copies ran while one was open for 4% of the time, Pallas kernels for 0%

profile of v1, /device:TPU:225, one launch (start us, length us, event | category | flops | bytes accessed | tf_op | source)
XLA Modules:
  0.0 1635.0 jit_solution(15987375150177533768)
XLA Ops:
  6.5 2.1 reduce_sum.18
  10.6 1.7 broadcast_multiply_fusion.3
  12.3 2.8 reshape.391
  15.1 2.5 convolution_bitcast_fusion.3
  18.0 1.7 broadcast_multiply_fusion
  19.7 2.6 broadcast_multiply_fusion.2
  22.9 3.4 mul.353
  26.3 3.4 mul.364
  29.7 3.4 mul.374
  33.8 688.4 %all-reduce.3.cloned.1.call-done = f32[4,5120]{1,0:T(4,128)} async-done(((f32[4,5120]{1,0:T(4,128)}), f32[4,5120]{1,0:T(4,128)}) %all-reduce.3.cloned.1.call-update) | async-done | bytes 81936 | tf_op jit(solution)/shard_map/psum | solution.py:97
  722.2 2.3 fusion.78
  725.1 12.2 all-to-all-start
  738.2 6.5 all-to-all-done
  745.3 2.5 bitcast_add_fusion.5
  749.2 1.6 convolution_bitcast_fusion.1
  753.0 2.0 collective-permute-start.2
  755.0 9.3 collective-permute-start.3
  765.6 2.0 copy.62
  767.6 3.3 collective-permute-start.4
  770.9 2.0 copy.63
  773.0 2.1 collective-permute-start.5
  775.0 2.1 fusion.75
  779.6 4.6 fusion.9
  784.2 5.0 collective-permute-start.1
  790.4 1.9 copy.65
  792.3 2.1 pad_maximum_fusion.4
  803.1 9.2 concatenate.27
  812.3 2.4 fusion.79
  814.7 4.2 fusion.76
  820.0 711.7 %all-reduce.5.cloned.1.call-done = f32[4,5120]{1,0:T(4,128)} async-done(((f32[4,5120]{1,0:T(4,128)}), f32[4,5120]{1,0:T(4,128)}) %all-reduce.5.cloned.1.call-update) | async-done | bytes 81936 | tf_op jit(solution)/shard_map/psum | solution.py:97
  1531.7 2.3 fusion.80
  1534.6 12.7 all-to-all-start.1
  1547.4 3.8 convolution_bitcast_fusion.2
  1551.2 1.8 copy.68
  1555.2 3.5 bitcast_add_fusion.2
  1563.1 2.3 collective-permute-start.8
  1565.4 9.0 collective-permute-start.9
  1579.6 3.3 collective-permute-start.10
  1584.4 1.9 collective-permute-start.11
  1586.3 6.2 fusion.12
  1592.5 5.2 collective-permute-start.7
  1600.1 2.0 pad_maximum_fusion.5
  1604.5 3.3 collective-permute-done.6
  1612.6 3.3 concatenate.31
  1615.9 4.3 fusion.81
  1620.2 1.8 copy.86
  1622.0 3.6 fusion
  1625.6 2.4 copy.87
  (161 shorter events, 46.9 us)
Async XLA Ops:
  6.5 715.7 %copy-start = (f32[80,5120]{1,0:T(8,128)S(1)}, f32[80,5120]{1,0:T(8,128)}, u32[]{:S(2)}) copy-start(f32[80,5120]{1,0:T(8,128)} %param.16) | copy-start | bytes 4915204
  6.5 3.9 copy-start.22
  6.5 715.7 %all-reduce.3.cloned.1.call-start = ((), (), s32[]{:S(2)}) async-start(), calls=%async_computation.2 | async-start | bytes 163840 | tf_op jit(solution)/shard_map/psum | solution.py:97
  15.1 3.0 copy-start.14
  15.1 2.6 copy-start.23
  15.1 2.9 copy-start.27
  29.7 707.8 %copy-start.36 = (f32[3,5]{1,0:T(4,128)S(1)}, f32[3,5]{1,0:T(4,128)}, u32[]{:S(2)}) copy-start(f32[3,5]{1,0:T(4,128)} %param.12) | copy-start | bytes 184
  33.2 711.7 %copy-start.37 = (s32[1,1,128]{2,1,0:T(1,128)S(1)}, s32[1,1,128]{2,1,0:T(1,128)}, u32[]{:S(2)}) copy-start(s32[1,1,128]{2,1,0:T(1,128)} %param.15) | copy-start | bytes 1540
  33.2 712.1 %copy-start.24 = (f32[5,5]{1,0:T(8,128)S(1)}, f32[5,5]{1,0:T(8,128)}, u32[]{:S(2)}) copy-start(f32[5,5]{1,0:T(8,128)} %param.14) | copy-start | bytes 304
  725.1 19.6 %all-to-all-start = ((f32[64,4,80]{2,1,0:T(4,128)}), f32[64,4,80]{2,1,0:T(4,128)S(1)}, u32[]{:S(2)}, u32[]{:S(2)}) async-start(f32[64,4,80]{2,1,0:T(4,128)} %stack.16), calls=%async_computation | async-start | bytes 262144 | tf_op jit(solution)/shard_map/all_to_all | solution.py:102
  737.3 794.4 %all-reduce.5.cloned.1.call-start = ((), (), s32[]{:S(2)}) async-start(), calls=%async_computation.3 | async-start | bytes 163840 | tf_op jit(solution)/shard_map/psum | solution.py:97
  738.1 63.6 %copy-start.25 = (f32[5]{0:T(128)}, f32[5]{0:T(128)S(1)}, u32[]{:S(2)}) copy-start(f32[5]{0:T(128)S(1)} %get-tuple-element.63) | copy-start | bytes 64
  738.1 63.6 %copy-start.28 = (f32[5]{0:T(128)}, f32[5]{0:T(128)S(1)}, u32[]{:S(2)}) copy-start(f32[5]{0:T(128)S(1)} %get-tuple-element.62) | copy-start | bytes 64
  745.3 3.9 copy-start.12
  751.8 13.8 copy-start.6
  751.8 13.8 copy-start.9
  751.8 13.8 copy-start.10
  753.0 41.5 %collective-permute-start.2 = (f32[2,4,5,25,1,1,128]{6,1,5,4,3,2,0:T(4,128)}, f32[2,4,5,25,1,1,128]{6,1,5,4,3,2,0:T(4,128)}, u32[]{:S(2)}, u32[]{:S(2)}) collective-permute-start(f32[2,4,5,25,1,1,128]{6,1,5,4,3,2,0:T(4,128)} %copy.58), channel_id=1, source_target_pairs={{0,8},{8,16},{16,24},{24,32},{32,40},{40,48},{48,56},{1,9},{9,17},... | collective-permute-start | bytes 1536008 | tf_op jit(solution)/shard_map/ppermute | solution.py:17
  755.0 40.7 %collective-permute-start.3 = (f32[2,4,5,25,1,1,128]{6,1,5,4,3,2,0:T(4,128)}, f32[2,4,5,25,1,1,128]{6,1,5,4,3,2,0:T(4,128)}, u32[]{:S(2)}, u32[]{:S(2)}) collective-permute-start(f32[2,4,5,25,1,1,128]{6,1,5,4,3,2,0:T(4,128)} %copy.58), channel_id=1, source_target_pairs={{8,0},{16,8},{24,16},{32,24},{40,32},{48,40},{56,48},{9,1},{17,9},... | collective-permute-start | bytes 1536008 | tf_op jit(solution)/shard_map/ppermute | solution.py:18
  767.6 16.6 %collective-permute-start.4 = (f32[2,4,5,25,1,1,1]{3,1,6,5,4,2,0:T(4,128)}, f32[2,4,5,25,1,1,1]{3,1,6,5,4,2,0:T(4,128)S(1)}, u32[]{:S(2)}, u32[]{:S(2)}) collective-permute-start(f32[2,4,5,25,1,1,1]{3,1,6,5,4,2,0:T(4,128)} %copy.62), channel_id=1, source_target_pairs={{0,1},{1,2},{2,3},{3,4},{4,5},{5,6},{6,7},{8,9},{9,10},{10,11},{11... | collective-permute-start | bytes 12008 | tf_op jit(solution)/shard_map/ppermute | solution.py:17
  772.9 6.6 copy-start.4
  772.9 6.6 copy-start.16
  772.9 6.6 copy-start.18
  772.9 6.6 copy-start.20
  772.9 6.6 copy-start.32
  772.9 6.6 copy-start.34
  772.9 6.6 copy-start.35
  773.0 17.4 %collective-permute-start.5 = (f32[2,4,5,25,1,1,1]{3,1,6,5,4,2,0:T(4,128)}, f32[2,4,5,25,1,1,1]{3,1,6,5,4,2,0:T(4,128)}, u32[]{:S(2)}, u32[]{:S(2)}) collective-permute-start(f32[2,4,5,25,1,1,1]{3,1,6,5,4,2,0:T(4,128)} %copy.63), channel_id=1, source_target_pairs={{1,0},{2,1},{3,2},{4,3},{5,4},{6,5},{7,6},{9,8},{10,9},{11,10},{12... | collective-permute-start | bytes 12008 | tf_op jit(solution)/shard_map/ppermute | solution.py:18
  778.2 19.5 %collective-permute-start = (f32[2,4,5,25,1,1,128]{6,1,5,4,3,2,0:T(4,128)}, f32[2,4,5,25,1,1,128]{6,1,5,4,3,2,0:T(4,128)}, u32[]{:S(2)}, u32[]{:S(2)}) collective-permute-start(f32[2,4,5,25,1,1,128]{6,1,5,4,3,2,0:T(4,128)} %copy.52), channel_id=1, source_target_pairs={{0,64},{64,128},{128,192},{1,65},{65,129},{129,193},{2,66},{66,130... | collective-permute-start | bytes 1536008 | tf_op jit(solution)/shard_map/ppermute | solution.py:17
  784.2 15.1 collective-permute-start.1
  794.5 4.4 copy-start.7
  812.3 2.4 copy-start.5
  814.7 4.2 copy-start.38
  818.9 728.4 %copy-start.15 = (f32[125,125,1,1]{1,0,2,3:T(8,128)S(1)}, f32[125,125,1,1]{1,0,2,3:T(8,128)}, u32[]{:S(2)}) copy-start(f32[125,125,1,1]{1,0,2,3:T(8,128)} %copy-done.14) | copy-start | bytes 187504
  1534.6 20.0 %all-to-all-start.1 = ((f32[64,4,80]{2,1,0:T(4,128)}), f32[64,4,80]{2,1,0:T(4,128)S(1)}, u32[]{:S(2)}, u32[]{:S(2)}) async-start(f32[64,4,80]{2,1,0:T(4,128)} %stack.20), calls=%async_computation.1 | async-start | bytes 262144 | tf_op jit(solution)/shard_map/all_to_all | solution.py:102
  1555.2 4.8 copy-start.13
  1561.9 15.0 copy-start.8
  1563.1 39.2 %collective-permute-start.8 = (f32[2,4,5,25,1,1,128]{6,1,5,4,3,2,0:T(4,128)}, f32[2,4,5,25,1,1,128]{6,1,5,4,3,2,0:T(4,128)}, u32[]{:S(2)}, u32[]{:S(2)}) collective-permute-start(f32[2,4,5,25,1,1,128]{6,1,5,4,3,2,0:T(4,128)} %copy.78), channel_id=1, source_target_pairs={{0,8},{8,16},{16,24},{24,32},{32,40},{40,48},{48,56},{1,9},{9,17},... | collective-permute-start | bytes 1536008 | tf_op jit(solution)/shard_map/ppermute | solution.py:17
  1565.4 38.0 %collective-permute-start.9 = (f32[2,4,5,25,1,1,128]{6,1,5,4,3,2,0:T(4,128)}, f32[2,4,5,25,1,1,128]{6,1,5,4,3,2,0:T(4,128)}, u32[]{:S(2)}, u32[]{:S(2)}) collective-permute-start(f32[2,4,5,25,1,1,128]{6,1,5,4,3,2,0:T(4,128)} %copy.78), channel_id=1, source_target_pairs={{8,0},{16,8},{24,16},{32,24},{40,32},{48,40},{56,48},{9,1},{17,9},... | collective-permute-start | bytes 1536008 | tf_op jit(solution)/shard_map/ppermute | solution.py:18
  1575.6 32.3 %collective-permute-start.6 = (f32[2,4,5,25,1,1,128]{6,1,5,4,3,2,0:T(4,128)}, f32[2,4,5,25,1,1,128]{6,1,5,4,3,2,0:T(4,128)}, u32[]{:S(2)}, u32[]{:S(2)}) collective-permute-start(f32[2,4,5,25,1,1,128]{6,1,5,4,3,2,0:T(4,128)} %copy.73), channel_id=1, source_target_pairs={{0,64},{64,128},{128,192},{1,65},{65,129},{129,193},{2,66},{66,130... | collective-permute-start | bytes 1536008 | tf_op jit(solution)/shard_map/ppermute | solution.py:17
  1576.9 9.4 copy-start.17
  1576.9 9.4 copy-start.19
  1576.9 9.4 copy-start.21
  1576.9 9.4 copy-start.33
  1579.6 12.9 collective-permute-start.10
  1584.4 14.6 collective-permute-start.11
  1592.5 16.9 %collective-permute-start.7 = (f32[2,4,5,25,1,1,128]{6,1,5,4,3,2,0:T(4,128)}, f32[2,4,5,25,1,1,128]{6,1,5,4,3,2,0:T(4,128)}, u32[]{:S(2)}, u32[]{:S(2)}) collective-permute-start(f32[2,4,5,25,1,1,128]{6,1,5,4,3,2,0:T(4,128)} %copy.73), channel_id=1, source_target_pairs={{64,0},{128,64},{192,128},{65,1},{129,65},{193,129},{66,2},{130,66... | collective-permute-start | bytes 1536008 | tf_op jit(solution)/shard_map/ppermute | solution.py:18
  1622.0 6.0 copy-start.1
  (7 other events, 7.0 us)
Sparse Core Ops, SparseCore 0:
  10.5 711.6 all-reduce.2
  820.1 711.5 all-reduce.4
